TPU v7x, 256 devices: a whole 4x4x8 slice. The times are simulated.
256 devices in a mesh: wide: 64 (over y, z, core), seq: 4 (over x).
Axes of the slice: x: 4, y: 4, z: 8, core: 2. Of those that a mesh axis runs over, the one named last changes fastest.
Arguments:
- power: bfloat16 [160, 2097152], P('seq', 'wide')
- bin_index: int32 [160], P('seq'), may hold values from 0 to 7, as said below
- session: int32 [16384], replicated, may hold values from 0 to 63, as said below
- readin_weight: bfloat16 [64, 128, 2048], P('wide'), may hold values from -0.5 to 0.5
- qkv_weight: bfloat16 [2048, 1536], replicated, may hold values from -0.125 to 0.125
Outputs:
- heads: bfloat16 [16384, 8, 1024], P(('wide', 'seq'))
Inputs may be any that keep to these rules, and one draw needn't show every extreme that they name: `bin_index`: the samples j * 40 to (j + 1) * 40 - 1 name only bins j * 2 to (j + 1) * 2 - 1. In each aligned block of 64 patches (patches k * 64 to (k + 1) * 64 - 1) no session is named by more than 2 patches; one session, the same for every block, is named by exactly 2 patches of every block.
All inputs are finite; a program needn't handle non-finite values.
Results may differ from a plain program's by a relative error of at most 0.008.
Values may be sent and summed in bfloat16 or wider, within the bound.
No kernel may reach another device: no remote copies, remote signals or barrier semaphores. Data moves between devices by JAX's collectives and lax.ppermute only.
A program may use at most 64 MiB of HBM per device.

v0:
```python
import jax
import jax.numpy as jnp
from jax import lax
from jax.sharding import PartitionSpec as P

CH = 128
HD = 128
HEADS = 8
KVH = 2
SPB = 20


def attention_heads(qkv_rows):
    row_count = qkv_rows.shape[0]
    length = qkv_rows.shape[1]
    group_size = HEADS // KVH
    values = qkv_rows.astype(jnp.float32)
    queries = values[:, :, : HEADS * HD].reshape(row_count, length, KVH, group_size, HD)
    key_rows = values[:, :, HEADS * HD : (HEADS + KVH) * HD].reshape(row_count, length, KVH, HD)
    value_rows = values[:, :, (HEADS + KVH) * HD :].reshape(row_count, length, KVH, HD)
    queries = queries / jnp.sqrt(jnp.mean(queries * queries, axis=-1, keepdims=True) + 1e-06)
    key_rows = key_rows / jnp.sqrt(jnp.mean(key_rows * key_rows, axis=-1, keepdims=True) + 1e-06)
    scores = jnp.einsum("pigrd,pjgd->pgrij", queries, key_rows) / HD**0.5
    exponent = jnp.exp(scores)
    weights = (exponent / jnp.sum(exponent, axis=-1, keepdims=True)).astype(jnp.bfloat16)
    mixed = jnp.einsum("pgrij,pjgd->pigrd", weights.astype(jnp.float32), value_rows)
    return mixed.reshape(row_count, length, HEADS * HD).astype(jnp.bfloat16)


def project_rows(tokens, qkv_weight):
    product = jnp.dot(
        tokens.reshape(-1, tokens.shape[-1]), qkv_weight, preferred_element_type=jnp.float32
    )
    return product.astype(jnp.bfloat16).reshape(tokens.shape[:-1] + (qkv_weight.shape[1],))


def readin_rows(slab, weight_block):
    tokens = jnp.einsum(
        "abtc,cd->abtd", slab, weight_block, preferred_element_type=jnp.float32
    ).astype(jnp.bfloat16)
    return tokens


def slot_ranks(owner_ids, wide_count):
    owner_marks = (owner_ids[..., None] == jnp.arange(wide_count, dtype=jnp.int32)).astype(
        jnp.int32
    )
    running = jnp.cumsum(owner_marks, axis=-2)
    return jnp.sum(owner_marks * running, axis=-1) - 1


def body(power, bin_index, session, readin_weight, qkv_weight):
    wide_count = lax.axis_size("wide")
    seq_count = lax.axis_size("seq")
    wide_index = lax.axis_index("wide")
    seq_index = lax.axis_index("seq")
    sample_rows, channels = power.shape
    patch_count = channels // CH
    quarter = patch_count // seq_count
    bin_count = sample_rows // SPB
    capacity = max(2, 2 * quarter // wide_count)
    signal = power.astype(jnp.float32)
    squares = lax.psum(jnp.sum(signal * signal, axis=0), "seq")
    inv_rms = 1.0 / jnp.sqrt(squares / (sample_rows * seq_count) + 1e-06)
    active = jnp.maximum(signal * inv_rms[None, :] - 0.8, 0.0)
    local_bins = bin_index - seq_index * bin_count
    onehot = (local_bins[:, None] == jnp.arange(bin_count, dtype=jnp.int32)[None, :]).astype(
        jnp.float32
    )
    binned = (jnp.dot(onehot.T, active, precision=lax.Precision.HIGHEST) * (1.0 / SPB)).astype(
        jnp.bfloat16
    )
    patches = binned.reshape(bin_count, patch_count, CH).transpose(1, 0, 2)
    owners = lax.dynamic_slice_in_dim(session, wide_index * patch_count, patch_count)
    weight_block = readin_weight[0]
    owner_grid = owners.reshape(seq_count, quarter)
    slot_rank = slot_ranks(owner_grid, wide_count)
    quarter_ids = jnp.arange(seq_count, dtype=jnp.int32)[:, None]
    slot_index = ((owner_grid * seq_count + quarter_ids) * capacity + slot_rank).reshape(
        patch_count
    )
    slot_count = seq_count * capacity
    length = patches.shape[1]
    outgoing = (
        jnp.zeros((wide_count * slot_count, length, CH), jnp.bfloat16).at[slot_index].set(patches)
    )
    outgoing = outgoing.reshape(wide_count, slot_count, length, CH)
    returned_rows = lax.all_to_all(
        readin_rows(
            lax.all_to_all(outgoing, "wide", split_axis=0, concat_axis=0, tiled=True), weight_block
        ),
        "wide",
        split_axis=0,
        concat_axis=0,
        tiled=True,
    )
    arrived = returned_rows.reshape(
        wide_count * slot_count, returned_rows.shape[2], returned_rows.shape[3]
    )[slot_index]
    arrived = lax.all_to_all(arrived, "seq", split_axis=0, concat_axis=1, tiled=True)
    projected = project_rows(arrived, qkv_weight)
    return attention_heads(projected)


def solution(mesh):
    placed = (P("seq", "wide"), P("seq"), P(), P("wide", None, None), P())
    return jax.shard_map(
        body, mesh=mesh, in_specs=placed, out_specs=P(("wide", "seq"), None, None), check_vma=False
    )
```

profile of v0, /device:TPU:1, one launch (start us, length us, event | category | flops | bytes accessed | tf_op | source)
XLA Modules:
  0.0 287.6 jit_solution(8272917020949830205)
XLA Ops:
  6.5 3.3 %fusion.1 = f32[32768]{0:T(1024)} fusion(bf16[40,32768]{1,0:T(8,128)(2,1)} %param.5), kind=kLoop, calls=%fused_computation.6 | loop fusion | flops 3899392 | bytes 2752512 | tf_op jit(solution)/shard_map/reduce_sum | solution.py:63
  9.8 0.8 dynamic_slice.3
  10.9 0.1 reduce_window_sum.11
  11.0 0.2 select_reduce_fusion
  11.3 0.8 compare_select_fusion
  12.1 46.1 %all-reduce.2.cloned.1.call-done = f32[32768]{0:T(1024)} async-done(((f32[32768]{0:T(1024)}), f32[32768]{0:T(1024)}) %all-reduce.2.cloned.1.call-update) | async-done | bytes 131088 | tf_op jit(solution)/shard_map/psum | solution.py:63
  58.2 0.9 add_rsqrt_fusion
  59.2 2.5 fusion.11
  61.7 0.1 broadcast_in_dim.4
  61.8 7.3 %scatter_fusion = bf16[512,2,128]{2,1,0:T(2,128)(2,1)S(1)} fusion(bf16[512,2,128]{2,1,0:T(2,128)(2,1)S(1)} %broadcast_in_dim.4, s32[256]{0:T(256)S(1)} %compare_select_fusion, bf16[256,2,128]{2,1,0:T(2,128)(2,1)S(1)} %fusion.11), kind=kCustom, calls=%fused_computation.1 | custom fusion | bytes 394240 | tf_op jit(solution)/shard_map/scatter | solution.py:85
  69.1 24.5 %all_to_all.25 = bf16[64,8,2,128]{3,1,2,0:T(8,128)(2,1)S(1)} all-to-all(bf16[64,8,2,128]{3,1,2,0:T(8,128)(2,1)S(1)} %copy.33), channel_id=1, replica_groups=mesh['wide'=64,'seq'=4] {'wide'}, dimensions={0} | all-to-all | bytes 524288 | tf_op jit(solution)/shard_map/all_to_all | solution.py:90
  93.7 3.2 %convolution_convert_fusion = bf16[64,8,2,2048]{3,1,2,0:T(8,128)(2,1)} fusion(bf16[64,8,2,128]{3,1,2,0:T(8,128)(2,1)S(1)} %all_to_all.25, bf16[1,128,2048]{2,1,0:T(8,128)(2,1)S(1)} %copy-done), kind=kOutput, calls=%fused_computation.10 | convolution fusion | flops 538968064 | bytes 4980736 | tf_op jit(solution)/shard_map/abtc,cd->abtd/dot_general | solution.py:38
  96.9 6.2 %all-to-all-start.1 = ((bf16[64,8,2,2048]{3,1,2,0:T(8,128)(2,1)}), bf16[64,8,2,2048]{3,1,2,0:T(8,128)(2,1)}, u32[]{:S(2)}, u32[]{:S(2)}) async-start(bf16[64,8,2,2048]{3,1,2,0:T(8,128)(2,1)} %convolution_convert_fusion), calls=%async_computation.1 | async-start | bytes 8388608 | tf_op jit(solution)/shard_map/all_to_all | solution.py:88
  103.1 95.8 %all-to-all-done.1 = bf16[64,8,2,2048]{3,1,2,0:T(8,128)(2,1)} async-done(((bf16[64,8,2,2048]{3,1,2,0:T(8,128)(2,1)}), bf16[64,8,2,2048]{3,1,2,0:T(8,128)(2,1)}, u32[]{:S(2)}, u32[]{:S(2)}) %all-to-all-start.1) | async-done | bytes 4194336 | tf_op jit(solution)/shard_map/all_to_all | solution.py:88
  198.9 2.5 copy.50
  201.4 6.2 %copy.35 = bf16[512,2,2048]{2,1,0:T(2,128)(2,1)} copy(bf16[512,2,2048]{2,0,1:T(8,128)(2,1)S(1)} %bitcast.54) | data formatting | bytes 8388608 | tf_op jit(solution)/shard_map/reshape | solution.py:97
  207.7 12.7 %gather_fusion = bf16[256,2,2048]{2,1,0:T(2,128)(2,1)S(1)} fusion(bf16[512,2,2048]{2,1,0:T(2,128)(2,1)} %copy.35, s32[1024]{0:T(1024)S(1)} %pad_clamp_fusion), kind=kCustom, calls=%fused_computation | custom fusion | bytes 4195328 | tf_op jit(solution)/shard_map/gather | solution.py:97
  220.4 28.8 %all_to_all.26 = bf16[256,2,2048]{2,1,0:T(2,128)(2,1)S(1)} all-to-all(bf16[256,2,2048]{2,1,0:T(2,128)(2,1)S(1)} %gather_fusion), channel_id=1, replica_groups=mesh['wide'=64,'seq'=4] {'seq'}, dimensions={0} | all-to-all | bytes 4194304 | tf_op jit(solution)/shard_map/all_to_all | solution.py:100
  249.3 2.5 copy.51
  251.8 2.2 reshape.56
  254.0 8.0 %fusion.24 = (f32[64,8,1536]{2,1,0:T(8,128)S(1)}, bf16[64,8,1536]{2,1,0:T(8,128)(2,1)}) fusion(bf16[512,2048]{1,0:T(8,128)(2,1)} %reshape.56, bf16[2048,1536]{1,0:T(8,128)(2,1)} %param.9), kind=kOutput, calls=%fused_computation.48 | convolution fusion | flops 3222798336 | bytes 13107200 | tf_op jit(solution)/shard_map/dot_general | solution.py:31
  262.0 1.7 copy-done.2
  263.7 0.3 multiply_reduce_fusion.1
  264.1 0.1 copy.38
  264.2 1.5 slice.16
  265.6 0.8 multiply_reduce_fusion
  266.5 0.1 copy.39
  266.6 0.2 copy.40
  266.8 7.2 %fusion.9 = f32[64,2,8,8,4]{3,2,4,1,0:T(8,128)} fusion(f32[64,8,2,4,128]{4,1,3,2,0:T(8,128)S(1)} %bitcast.56, f32[64,8,2,4]{1,3,2,0:T(4,128)S(1)} %copy.40, f32[64,8,1536]{2,1,0:T(8,128)} %copy-done.2, f32[64,8,2]{1,2,0:T(2,128)S(1)} %copy.38), kind=kOutput, calls=%fused_computation.17 | convolution fusion | flops 9043968 | bytes 2772992 | tf_op jit(solution)/shard_map/pigrd,pjgd->pgrij/dot_general | solution.py:23
  274.0 2.7 copy.41
  276.9 1.6 copy.42
  278.4 2.3 convolution_convert_fusion.2
  (23 shorter events, 0.7 us)
Async XLA Ops:
  6.5 87.1 %copy-start = (bf16[1,128,2048]{2,1,0:T(8,128)(2,1)S(1)}, bf16[1,128,2048]{2,1,0:T(8,128)(2,1)}, u32[]{:S(2)}) copy-start(bf16[1,128,2048]{2,1,0:T(8,128)(2,1)} %param.8) | copy-start | bytes 1572868
  6.5 52.6 %copy-start.1 = (bf16[40,32768]{1,0:T(8,128)(2,1)S(1)}, bf16[40,32768]{1,0:T(8,128)(2,1)}, u32[]{:S(2)}) copy-start(bf16[40,32768]{1,0:T(8,128)(2,1)} %param.5) | copy-start | bytes 7864324
  6.5 5.6 %copy-start.3 = (s32[40]{0:T(128)S(1)}, s32[40]{0:T(128)}, u32[]{:S(2)}) copy-start(s32[40]{0:T(128)} %param.6) | copy-start | bytes 484
  6.5 51.7 %all-reduce.2.cloned.1.call-start = ((), (), s32[]{:S(2)}) async-start(), calls=%async_computation.3 | async-start | bytes 262144 | tf_op jit(solution)/shard_map/psum | solution.py:63
  96.9 102.1 %all-to-all-start.1 = ((bf16[64,8,2,2048]{3,1,2,0:T(8,128)(2,1)}), bf16[64,8,2,2048]{3,1,2,0:T(8,128)(2,1)}, u32[]{:S(2)}, u32[]{:S(2)}) async-start(bf16[64,8,2,2048]{3,1,2,0:T(8,128)(2,1)} %convolution_convert_fusion), calls=%async_computation.1 | async-start | bytes 8388608 | tf_op jit(solution)/shard_map/all_to_all | solution.py:88
  262.0 1.7 copy-start.2
Sparse Core Ops, SparseCore 0:
  10.0 48.2 all-reduce.1
where the time goes:
time: 288 us
  waiting for transfers between devices  142 us (49%)
  blocking collectives  53.4 us (19%)
  local copies, waits for them, and re-layouts  42.5 us (15%)
  matrix products  23.3 us (8%)
  between operations  13.6 us (5%)
  other arithmetic  6.75 us (2%)
  starting transfers between devices  6.24 us (2%)
    all_to_all x1, waiting for transfers between devices, body(): lax.all_to_all(readin_rows(lax.all_to_all(outgoing, 'wide', split_axis=0,...  95.8 us
    psum x1, waiting for transfers between devices, body(): squares = lax.psum(jnp.sum(signal * signal, axis=0), 'seq')  46.1 us
    all_to_all x1, blocking collectives, body(): lax.all_to_all(arrived, 'seq', split_axis=0, concat_axis=1, tiled=True)  28.8 us
    all_to_all x1, blocking collectives, body(): lax.all_to_all(outgoing, 'wide', split_axis=0, concat_axis=0, tiled=True)  24.5 us
    gather x1, local copies, waits for them, and re-layouts, body(): returned_rows.reshape(wide_count * slot_count, returned_rows.shape[2], re...  12.7 us
    dot_general x1, matrix products, project_rows(): jnp.dot(tokens.reshape(-1, tokens.shape[-1]), qkv_weight, preferred_eleme...  8.04 us
    scatter x1, local copies, waits for them, and re-layouts, body(): jnp.zeros((wide_count * slot_count, length, CH), jnp.bfloat16)  7.27 us
    dot_general x1, matrix products, attention_heads(): scores = jnp.einsum('pigrd,pjgd->pgrij', queries, key_rows) / HD ** 0.5  7.2 us
  transfers between devices with their start and end apart: 2, of which 2 were waited for; matrix products, arithmetic and copies ran while one was open for 1% of the time, Pallas kernels for 0%

commit v1 on v0

--- a/solution.py
+++ b/solution.py
@@ -60,7 +60,7 @@
     bin_count = sample_rows // SPB
     capacity = max(2, 2 * quarter // wide_count)
     signal = power.astype(jnp.float32)
-    squares = lax.psum(jnp.sum(signal * signal, axis=0), "seq")
+    squares = jnp.sum(lax.all_gather(jnp.sum(signal * signal, axis=0), "seq"), axis=0)
     inv_rms = 1.0 / jnp.sqrt(squares / (sample_rows * seq_count) + 1e-06)
     active = jnp.maximum(signal * inv_rms[None, :] - 0.8, 0.0)
     local_bins = bin_index - seq_index * bin_count

time: 288 us -> 246 us (0.85)
  waiting for transfers between devices: 142 us -> 95.8 us
  blocking collectives: 53.4 us -> 68.6 us
  between operations: 13.6 us -> 0.18 us
    psum x1 -> x0, waiting for transfers between devices: 46.1 us -> none  [body(): squares = lax.psum(jnp.sum(signal * signal, axis=0), 'seq')]
    all_gather x0 -> x1, blocking collectives: none -> 12.8 us  [body(): lax.all_gather(jnp.sum(signal * signal, axis=0), 'seq')]
  transfers between devices with their start and end apart: 2 -> 1, of which waited for: 2 -> 1; matrix products, arithmetic and copies ran while one was open for 1% -> 0% of each run, Pallas kernels for 0% -> 0%
where the time goes in v1:
time: 246 us; the launch traced here: 245 us
  waiting for transfers between devices  95.8 us (39%)
  blocking collectives  68.6 us (28%)
  local copies, waits for them, and re-layouts  44.6 us (18%)
  matrix products  23.3 us (9%)
  other arithmetic  6.56 us (3%)
  starting transfers between devices  6.24 us (3%)
    all_to_all x1, waiting for transfers between devices, body(): lax.all_to_all(readin_rows(lax.all_to_all(outgoing, 'wide', split_axis=0,...  95.8 us
    all_to_all x1, blocking collectives, body(): lax.all_to_all(arrived, 'seq', split_axis=0, concat_axis=1, tiled=True)  29.8 us
    all_to_all x1, blocking collectives, body(): lax.all_to_all(outgoing, 'wide', split_axis=0, concat_axis=0, tiled=True)  26 us
    all_gather x1, blocking collectives, body(): lax.all_gather(jnp.sum(signal * signal, axis=0), 'seq')  12.8 us
    gather x1, local copies, waits for them, and re-layouts, body(): returned_rows.reshape(wide_count * slot_count, returned_rows.shape[2], re...  12.7 us
    dot_general x1, matrix products, project_rows(): jnp.dot(tokens.reshape(-1, tokens.shape[-1]), qkv_weight, preferred_eleme...  8.04 us
    scatter x1, local copies, waits for them, and re-layouts, body(): jnp.zeros((wide_count * slot_count, length, CH), jnp.bfloat16)  7.27 us
    dot_general x1, matrix products, attention_heads(): scores = jnp.einsum('pigrd,pjgd->pgrij', queries, key_rows) / HD ** 0.5  7.2 us
  transfers between devices with their start and end apart: 1, of which 1 were waited for; matrix products, arithmetic and copies ran while one was open for 0% of the time, Pallas kernels for 0%

profile of v1, /device:TPU:1, one launch (start us, length us, event | category | flops | bytes accessed | tf_op | source)
XLA Modules:
  0.0 245.2 jit_solution(1706037250768357711)
XLA Ops:
  0.0 0.8 dynamic_slice.3
  1.1 0.1 reduce_window_sum.11
  1.2 0.2 select_reduce_fusion
  1.6 2.6 %fusion.1 = f32[32768]{0:T(1024)S(1)} fusion(bf16[40,32768]{1,0:T(8,128)(2,1)} %param.5), kind=kLoop, calls=%fused_computation.6 | loop fusion | flops 3899392 | bytes 2752512 | tf_op jit(solution)/shard_map/reduce_sum | solution.py:63
  4.2 12.8 %all-gather = f32[131072]{0:T(1024)} all-gather(f32[32768]{0:T(1024)S(1)} %fusion.1), channel_id=2, replica_groups=mesh['wide'=64,'seq'=4] {'seq'}, dimensions={0}, use_global_device_ids=true | all-gather | bytes 655360 | tf_op jit(solution)/shard_map/all_gather | solution.py:63
  17.0 2.1 reshape.81
  19.0 1.4 reduce_sum.56
  20.5 0.8 compare_select_fusion
  21.2 2.5 %fusion.11 = bf16[256,2,128]{2,1,0:T(2,128)(2,1)S(1)} fusion(bf16[40,32768]{1,0:T(8,128)(2,1)S(1)} %copy-done.1, f32[32768]{0:T(1024)S(1)} %add_rsqrt_fusion, s32[40]{0:T(128)S(1)} %broadcast_subtract_fusion), kind=kOutput, calls=%fused_computation.21 | convolution fusion | flops 36831312 | bytes 2883744 | tf_op jit(solution)/shard_map/dot_general | solution.py:70
  23.7 0.1 broadcast_in_dim.4
  23.9 7.3 %scatter_fusion = bf16[512,2,128]{2,1,0:T(2,128)(2,1)S(1)} fusion(bf16[512,2,128]{2,1,0:T(2,128)(2,1)S(1)} %broadcast_in_dim.4, s32[256]{0:T(256)S(1)} %compare_select_fusion, bf16[256,2,128]{2,1,0:T(2,128)(2,1)S(1)} %fusion.11), kind=kCustom, calls=%fused_computation.1 | custom fusion | bytes 394240 | tf_op jit(solution)/shard_map/scatter | solution.py:85
  31.2 26.0 %all_to_all.25 = bf16[64,8,2,128]{3,1,2,0:T(8,128)(2,1)S(1)} all-to-all(bf16[64,8,2,128]{3,1,2,0:T(8,128)(2,1)S(1)} %copy.47), channel_id=1, replica_groups=mesh['wide'=64,'seq'=4] {'wide'}, dimensions={0} | all-to-all | bytes 524288 | tf_op jit(solution)/shard_map/all_to_all | solution.py:90
  57.2 3.2 %convolution_convert_fusion = bf16[64,8,2,2048]{3,1,2,0:T(8,128)(2,1)} fusion(bf16[64,8,2,128]{3,1,2,0:T(8,128)(2,1)S(1)} %all_to_all.25, bf16[1,128,2048]{2,1,0:T(8,128)(2,1)S(1)} %copy-done), kind=kOutput, calls=%fused_computation.10 | convolution fusion | flops 538968064 | bytes 4980736 | tf_op jit(solution)/shard_map/abtc,cd->abtd/dot_general | solution.py:38
  60.4 6.2 %all-to-all-start.1 = ((bf16[64,8,2,2048]{3,1,2,0:T(8,128)(2,1)}), bf16[64,8,2,2048]{3,1,2,0:T(8,128)(2,1)}, u32[]{:S(2)}, u32[]{:S(2)}) async-start(bf16[64,8,2,2048]{3,1,2,0:T(8,128)(2,1)} %convolution_convert_fusion), calls=%async_computation.1 | async-start | bytes 8388608 | tf_op jit(solution)/shard_map/all_to_all | solution.py:88
  66.7 95.8 %all-to-all-done.1 = bf16[64,8,2,2048]{3,1,2,0:T(8,128)(2,1)} async-done(((bf16[64,8,2,2048]{3,1,2,0:T(8,128)(2,1)}), bf16[64,8,2,2048]{3,1,2,0:T(8,128)(2,1)}, u32[]{:S(2)}, u32[]{:S(2)}) %all-to-all-start.1) | async-done | bytes 4194336 | tf_op jit(solution)/shard_map/all_to_all | solution.py:88
  162.5 2.5 %copy.64 = bf16[64,8,2,2048]{3,1,0,2:T(8,128)(2,1)S(1)} copy(bf16[64,8,2,2048]{3,1,2,0:T(8,128)(2,1)} %all-to-all-done.1) | data formatting | bytes 8388608 | tf_op jit(solution)/shard_map/all_to_all | solution.py:88
  165.0 6.2 %copy.49 = bf16[512,2,2048]{2,1,0:T(2,128)(2,1)} copy(bf16[512,2,2048]{2,0,1:T(8,128)(2,1)S(1)} %bitcast.54) | data formatting | bytes 8388608 | tf_op jit(solution)/shard_map/reshape | solution.py:97
  171.2 12.7 %gather_fusion = bf16[256,2,2048]{2,1,0:T(2,128)(2,1)S(1)} fusion(bf16[512,2,2048]{2,1,0:T(2,128)(2,1)} %copy.49, s32[1024]{0:T(1024)S(1)} %pad_clamp_fusion), kind=kCustom, calls=%fused_computation | custom fusion | bytes 4195328 | tf_op jit(solution)/shard_map/gather | solution.py:97
  184.0 29.8 %all_to_all.26 = bf16[256,2,2048]{2,1,0:T(2,128)(2,1)S(1)} all-to-all(bf16[256,2,2048]{2,1,0:T(2,128)(2,1)S(1)} %gather_fusion), channel_id=1, replica_groups=mesh['wide'=64,'seq'=4] {'seq'}, dimensions={0} | all-to-all | bytes 4194304 | tf_op jit(solution)/shard_map/all_to_all | solution.py:100
  213.8 2.5 %copy.65 = bf16[4,64,2,2048]{3,2,0,1:T(2,128)(2,1)S(1)} copy(bf16[4,64,2,2048]{3,2,1,0:T(2,128)(2,1)S(1)} %bitcast.57) | data formatting | bytes 4194304 | tf_op jit(solution)/shard_map/all_to_all | solution.py:100
  216.2 2.2 reshape.60
  218.5 8.0 %fusion.24 = (f32[64,8,1536]{2,1,0:T(8,128)S(1)}, bf16[64,8,1536]{2,1,0:T(8,128)(2,1)}) fusion(bf16[512,2048]{1,0:T(8,128)(2,1)} %reshape.60, bf16[2048,1536]{1,0:T(8,128)(2,1)} %param.9), kind=kOutput, calls=%fused_computation.48 | convolution fusion | flops 3222798336 | bytes 13107200 | tf_op jit(solution)/shard_map/dot_general | solution.py:31
  226.5 1.7 copy-done.2
  228.2 0.3 multiply_reduce_fusion.1
  228.6 1.5 slice.16
  230.1 0.8 multiply_reduce_fusion
  230.9 0.1 copy.53
  231.1 0.2 copy.54
  231.3 7.2 %fusion.9 = f32[64,2,8,8,4]{3,2,4,1,0:T(8,128)} fusion(f32[64,8,2,4,128]{4,1,3,2,0:T(8,128)S(1)} %bitcast.56, f32[64,8,2,4]{1,3,2,0:T(4,128)S(1)} %copy.54, f32[64,8,1536]{2,1,0:T(8,128)} %copy-done.2, f32[64,8,2]{1,2,0:T(2,128)S(1)} %copy.52), kind=kOutput, calls=%fused_computation.17 | convolution fusion | flops 9043968 | bytes 2772992 | tf_op jit(solution)/shard_map/pigrd,pjgd->pgrij/dot_general | solution.py:23
  238.5 2.7 %copy.55 = f32[64,2,8,8,4]{0,2,3,4,1:T(8,128)S(1)} copy(f32[64,2,8,8,4]{3,2,4,1,0:T(8,128)} %fusion.9) | data formatting | bytes 262144 | tf_op jit(solution)/shard_map/pigrd,pjgd->pgrij/dot_general | solution.py:23
  241.3 1.6 copy.56
  242.9 2.3 convolution_convert_fusion.2
  (23 shorter events, 0.9 us)
Async XLA Ops:
  0.0 57.2 %copy-start = (bf16[1,128,2048]{2,1,0:T(8,128)(2,1)S(1)}, bf16[1,128,2048]{2,1,0:T(8,128)(2,1)}, u32[]{:S(2)}) copy-start(bf16[1,128,2048]{2,1,0:T(8,128)(2,1)} %param.8) | copy-start | bytes 1572868
  1.6 18.9 %copy-start.3 = (s32[40]{0:T(128)S(1)}, s32[40]{0:T(128)}, u32[]{:S(2)}) copy-start(s32[40]{0:T(128)} %param.6) | copy-start | bytes 484
  1.6 19.7 %copy-start.1 = (bf16[40,32768]{1,0:T(8,128)(2,1)S(1)}, bf16[40,32768]{1,0:T(8,128)(2,1)}, u32[]{:S(2)}) copy-start(bf16[40,32768]{1,0:T(8,128)(2,1)} %param.5) | copy-start | bytes 7864324
  60.4 102.1 %all-to-all-start.1 = ((bf16[64,8,2,2048]{3,1,2,0:T(8,128)(2,1)}), bf16[64,8,2,2048]{3,1,2,0:T(8,128)(2,1)}, u32[]{:S(2)}, u32[]{:S(2)}) async-start(bf16[64,8,2,2048]{3,1,2,0:T(8,128)(2,1)} %convolution_convert_fusion), calls=%async_computation.1 | async-start | bytes 8388608 | tf_op jit(solution)/shard_map/all_to_all | solution.py:88
  226.5 1.7 copy-start.2
